TPU v7x, 32 devices: a whole 2x2x4 slice. The times are simulated.
32 devices in a mesh: ctx: 8 (over y, x, core), tp: 4 (over z).
Axes of the slice: x: 2, y: 2, z: 4, core: 2. Of those that a mesh axis runs over, the one named last changes fastest.
Arguments:
- stream: bfloat16 [1024, 4096], P('ctx', 'tp'), may hold values from -52 to 52
- shutter: bfloat16 [1024, 4096], P('ctx', 'tp'), may hold values from -6 to 6
- feeder: bfloat16 [1024, 4096], P('ctx', 'tp'), may hold values from -6 to 6
- stencil: float32 [7, 4096], P(None, 'tp'), may hold values from -2 to 2
- valves: bfloat16 [1024, 4096], P('ctx', 'tp'), may hold values from -6 to 6
- intake: bfloat16 [1024, 4096], P('ctx', 'tp'), may hold values from -6 to 6
- kernel: float32 [128, 4096], P(None, 'tp'), may hold values from -0.5 to 0.5
- scaling: float32 [4096], P('tp'), may hold values from 0.1 to 1.9
- queries: bfloat16 [1024, 4096], P('ctx', 'tp'), may hold values from -87 to 87
- matchers: bfloat16 [1024, 4096], P('ctx', 'tp'), may hold values from -6 to 6
- segments: int32 [1024], replicated, may hold values from 0 to 3, never falling along the last dimension, each value on 1 to 768 neighbouring positions
- cotangent: bfloat16 [1024, 4096], P('ctx', 'tp'), may hold values from -6 to 6
Outputs:
- result: bfloat16 [1024, 4096], P('ctx', 'tp')
- stream_grad: bfloat16 [1024, 4096], P('ctx', 'tp')
- shutter_grad: bfloat16 [1024, 4096], P('ctx', 'tp')
- feeder_grad: bfloat16 [1024, 4096], P('ctx', 'tp')
- stencil_grad: float32 [7, 4096], P(None, 'tp')
- valves_grad: bfloat16 [1024, 4096], P('ctx', 'tp')
- intake_grad: bfloat16 [1024, 4096], P('ctx', 'tp')
- kernel_grad: float32 [128, 4096], P(None, 'tp')
- scaling_grad: float32 [4096], P('tp')
- queries_grad: bfloat16 [1024, 4096], P('ctx', 'tp')
- matchers_grad: bfloat16 [1024, 4096], P('ctx', 'tp')
Inputs may be any that keep to these rules, and one draw needn't show every extreme that they name: `segments`: document numbers never fall along the context; each of the 4 documents covers 1 to 768 positions, and one covers exactly 768.
All inputs are finite; a program needn't handle non-finite values.
Results may differ from a plain program's by a relative error of at most 0.03.
Values may be sent and summed in bfloat16 or wider, within the bound.
No kernel may reach another device: no remote copies, remote signals or barrier semaphores. Data moves between devices by JAX's collectives and lax.ppermute only.
A program may use at most 192 MiB of HBM per device.

v0:
```python
import math
import jax
import jax.numpy as jnp
from jax import lax
from jax.sharding import PartitionSpec as P

HD = 128
D = 4096
KS = 7
KM = 128
epsilon = 1e-06


def as_sent(shard):

    def short(part):
        return part.astype(jnp.bfloat16) if part.dtype == jnp.float32 else part

    return jax.tree.map(short, shard)


def passed_along(value, axis, steps):
    count = lax.axis_size(axis)
    leading, last = (max(0, -steps), min(count, count - steps))
    return lax.ppermute(value, axis, [(source, source + steps) for source in range(leading, last)])


def depthwise(padded, tap_rows):
    return lax.conv_general_dilated(
        padded[None],
        tap_rows[:, None, :],
        (1,),
        "VALID",
        dimension_numbers=("NWC", "WIO", "NWC"),
        feature_group_count=padded.shape[1],
        precision=lax.Precision.HIGHEST,
    )[0]


def neighbor_rows(edge_rows, offset):
    return passed_along(as_sent(edge_rows), "ctx", offset).astype(edge_rows.dtype)


def channel_total(partial_value):
    return lax.psum(partial_value, "tp")


def shards(
    stream,
    shutter,
    feeder,
    stencil,
    valves,
    intake,
    kernel,
    scaling,
    queries,
    matchers,
    segments,
    cotangent,
):
    local_rows = stream.shape[0]
    width_local = stream.shape[1]
    head_count = width_local // HD
    total_rows = local_rows * lax.axis_size("ctx")
    position = lax.axis_index("ctx") * local_rows
    scale_factor = 1.0 / math.sqrt(HD)
    widened = stream.astype(jnp.float32)
    inner_one = feeder.astype(jnp.float32) * widened
    rim_one = neighbor_rows(inner_one[local_rows - (KS - 1) :], 1)
    padded_one = jnp.concatenate([rim_one, inner_one], axis=0)
    conv_one = depthwise(padded_one, stencil[::-1])
    first_out = (widened + shutter.astype(jnp.float32) * conv_one).astype(jnp.bfloat16)
    first_wide = first_out.astype(jnp.float32)
    inner_two = intake.astype(jnp.float32) * first_wide
    rim_two = neighbor_rows(inner_two[local_rows - (KM - 1) :], 1)
    padded_two = jnp.concatenate([rim_two, inner_two], axis=0)
    conv_two = depthwise(padded_two, kernel[::-1])
    second_out = (first_wide + valves.astype(jnp.float32) * conv_two).astype(jnp.bfloat16)
    second_wide = second_out.astype(jnp.float32)
    squares = channel_total(jnp.sum(second_wide * second_wide, axis=1))
    inverse_rms = lax.rsqrt(squares / D + epsilon)
    normed = (second_wide * inverse_rms[:, None] * scaling).astype(jnp.bfloat16)
    keys_whole, values_whole = (
        lax.all_gather(matchers, "ctx", axis=0, tiled=True),
        lax.all_gather(normed, "ctx", axis=0, tiled=True),
    )
    query_pos = position + jnp.arange(local_rows, dtype=jnp.int32)
    key_pos = jnp.arange(total_rows, dtype=jnp.int32)
    query_seg = lax.dynamic_slice_in_dim(segments, position, local_rows, 0)
    visible = (key_pos[None, :] <= query_pos[:, None]) & (segments[None, :] == query_seg[:, None])
    contract = (((1,), (1,)), ((), ()))
    weight_list = []
    dscore_list = []
    attended_list = []
    query_grad_list = []
    logsum_list = []
    delta_list = []
    for head_index in range(head_count):
        columns = slice(head_index * HD, (head_index + 1) * HD)
        query_head = queries[:, columns]
        key_head = keys_whole[:, columns]
        value_head = values_whole[:, columns]
        cotangent_head = cotangent[:, columns]
        scores = (
            lax.dot_general(query_head, key_head, contract, preferred_element_type=jnp.float32)
            * scale_factor
        )
        scores = jnp.where(visible, scores, -jnp.inf)
        row_max = jnp.max(scores, axis=1)
        logsum = row_max + jnp.log(jnp.sum(jnp.exp(scores - row_max[:, None]), axis=1))
        weights = jnp.exp(scores - logsum[:, None]).astype(jnp.bfloat16)
        attended = jnp.dot(weights, value_head, preferred_element_type=jnp.float32)
        weight_grad = lax.dot_general(
            cotangent_head, value_head, contract, preferred_element_type=jnp.float32
        )
        row_delta = jnp.sum(cotangent_head.astype(jnp.float32) * attended, axis=1)
        dscore = (
            scale_factor * weights.astype(jnp.float32) * (weight_grad - row_delta[:, None])
        ).astype(jnp.bfloat16)
        query_grad = jnp.dot(dscore, key_head, preferred_element_type=jnp.float32)
        weight_list.append(weights)
        dscore_list.append(dscore)
        attended_list.append(attended)
        query_grad_list.append(query_grad)
        logsum_list.append(logsum)
        delta_list.append(row_delta)
    attended_all = jnp.concatenate(attended_list, axis=1)
    result = (second_wide + attended_all).astype(jnp.bfloat16)
    queries_grad = jnp.concatenate(query_grad_list, axis=1).astype(jnp.bfloat16)
    query_heads = queries.reshape(local_rows, head_count, HD)
    cotangent_heads = cotangent.reshape(local_rows, head_count, HD)
    weights_all = jnp.stack(weight_list)
    dscore_all = jnp.stack(dscore_list)
    dscore_part = lax.slice_in_dim(dscore_all, 0, local_rows * lax.axis_size("ctx"), axis=2)
    key_part = jnp.einsum(
        "hts,the->she", dscore_part, query_heads, preferred_element_type=jnp.float32
    )
    value_part = jnp.einsum(
        "hts,the->she", weights_all, cotangent_heads, preferred_element_type=jnp.float32
    )
    summed = lax.psum_scatter(
        jnp.concatenate(
            [
                key_part.reshape(local_rows * lax.axis_size("ctx"), width_local),
                value_part.reshape(local_rows * lax.axis_size("ctx"), width_local),
            ],
            axis=1,
        ).astype(jnp.bfloat16),
        "ctx",
        scatter_dimension=0,
        tiled=True,
    ).astype(jnp.float32)
    matchers_grad = summed[:, :width_local].astype(jnp.bfloat16)
    value_grad = summed[:, width_local:]
    gain_part = value_grad * scaling
    projected = channel_total(jnp.sum(gain_part * second_wide, axis=1))
    scaling_part = jnp.sum(value_grad * second_wide * inverse_rms[:, None], axis=0)
    second_grad = (
        cotangent.astype(jnp.float32)
        + inverse_rms[:, None] * gain_part
        - second_wide * (inverse_rms**3 * projected / D)[:, None]
    )
    valves_grad = (second_grad * conv_two).astype(jnp.bfloat16)
    dconv_two = second_grad * valves.astype(jnp.float32)
    back_two = neighbor_rows(dconv_two[: KM - 1], -1)
    dinner_two = depthwise(jnp.concatenate([dconv_two, back_two], axis=0), kernel)
    intake_grad = (dinner_two * first_wide).astype(jnp.bfloat16)
    kernel_part = depthwise(padded_two, dconv_two)[::-1]
    first_grad = second_grad + dinner_two * intake.astype(jnp.float32)
    shutter_grad = (first_grad * conv_one).astype(jnp.bfloat16)
    dconv_one = first_grad * shutter.astype(jnp.float32)
    back_one = neighbor_rows(dconv_one[: KS - 1], -1)
    dinner_one = depthwise(jnp.concatenate([dconv_one, back_one], axis=0), stencil)
    feeder_grad = (dinner_one * widened).astype(jnp.bfloat16)
    stencil_part = depthwise(padded_one, dconv_one)[::-1]
    stream_grad = (first_grad + dinner_one * feeder.astype(jnp.float32)).astype(jnp.bfloat16)
    stencil_sum, kernel_sum, scaling_sum = (
        lax.psum(stencil_part.astype(jnp.bfloat16), "ctx").astype(jnp.float32),
        lax.psum(kernel_part.astype(jnp.bfloat16), "ctx").astype(jnp.float32),
        lax.psum(scaling_part.astype(jnp.bfloat16), "ctx").astype(jnp.float32),
    )
    normalizer = math.sqrt(total_rows)
    return (
        result,
        stream_grad,
        shutter_grad,
        feeder_grad,
        stencil_sum / normalizer,
        valves_grad,
        intake_grad,
        kernel_sum / normalizer,
        scaling_sum / normalizer,
        queries_grad,
        matchers_grad,
    )


def solution(mesh):
    placed = (
        P("ctx", "tp"),
        P("ctx", "tp"),
        P("ctx", "tp"),
        P(None, "tp"),
        P("ctx", "tp"),
        P("ctx", "tp"),
        P(None, "tp"),
        P("tp"),
        P("ctx", "tp"),
        P("ctx", "tp"),
        P(),
        P("ctx", "tp"),
    )
    return jax.shard_map(
        shards,
        mesh=mesh,
        in_specs=placed,
        out_specs=(
            P("ctx", "tp"),
            P("ctx", "tp"),
            P("ctx", "tp"),
            P("ctx", "tp"),
            P(None, "tp"),
            P("ctx", "tp"),
            P("ctx", "tp"),
            P(None, "tp"),
            P("tp"),
            P("ctx", "tp"),
            P("ctx", "tp"),
        ),
        check_vma=False,
    )
```

profile of v0, /device:TPU:0, one launch (start us, length us, event | category | flops | bytes accessed | tf_op | source)
XLA Modules:
  0.0 272.9 jit_solution(10646670163490515569)
XLA Ops:
  9.1 2.4 collective-permute-start
  11.4 2.8 %rev.12 = f32[7,1024]{1,0:T(8,128)S(1)} reverse(f32[7,1024]{1,0:T(8,128)} %param.15), dimensions={0} | reverse | bytes 57344 | tf_op jit(solution)/shard_map/rev | solution.py:72
  18.3 4.5 %collective-permute-start.1 = (bf16[127,1024]{1,0:T(8,128)(2,1)}, bf16[127,1024]{1,0:T(8,128)(2,1)S(1)}, u32[]{:S(2)}, u32[]{:S(2)}) collective-permute-start(bf16[127,1024]{1,0:T(8,128)(2,1)} %slice.349), channel_id=1, source_target_pairs={{0,4},{4,8},{8,12},{12,16},{16,20},{20,24},{24,28},{1,5},{5,9},{9,... | collective-permute-start | bytes 780296 | tf_op jit(solution)/shard_map/ppermute | solution.py:25
  25.1 5.6 %fusion.74 = f32[1,128,1024]{2,0,1:T(1,128)S(1)} fusion(f32[1,255,1024]{2,0,1:T(1,128)S(1)} %broadcast_in_dim.33, f32[128,1,1024]{2,0,1:T(8,128)S(1)} %bitcast.165), kind=kOutput, calls=%fused_computation.133 | convolution fusion | flops 201326592 | bytes 2093056 | tf_op jit(solution)/shard_map/conv_general_dilated | solution.py:29
  31.6 11.9 %psum.35 = f32[128]{0:T(128)S(1)} all-reduce(f32[128]{0:T(128)S(1)} %get-tuple-element.63), channel_id=1, replica_groups=mesh['ctx'=8,'tp'=4] {'tp'}, use_global_device_ids=true, to_apply=%region_3.4 | all-reduce | flops 128 | bytes 1024 | tf_op jit(solution)/shard_map/psum | solution.py:45
  64.7 2.6 copy.116
  67.3 7.6 %all-gather.5.cloned.1.call-done = bf16[1024,1024]{1,0:T(8,128)(2,1)} async-done(((bf16[128,1024]{1,0:T(8,128)(2,1)}), bf16[1024,1024]{1,0:T(8,128)(2,1)}) %all-gather.5.cloned.1.call-update) | async-done | bytes 2097168 | tf_op jit(solution)/shard_map/all_gather | solution.py:86
  74.9 1.4 fusion.87
  91.7 2.6 copy.114
  94.3 4.7 %pad_maximum_fusion = bf16[1024,2048]{1,0:T(8,128)(2,1)} fusion(bf16[1024,1024]{1,0:T(8,128)(2,1)} %copy.116, bf16[1024,1024]{1,0:T(8,128)(2,1)} %copy.114), kind=kLoop, calls=%fused_computation | loop fusion | flops 8388608 | bytes 8388608 | tf_op jit(solution)/shard_map/concatenate | solution.py:143
  99.3 1.7 copy.68
  101.0 1.6 copy.67
  104.3 1.5 constant_dynamic-update-slice_fusion.7
  105.8 1.5 constant_dynamic-update-slice_fusion.6
  107.3 1.5 constant_dynamic-update-slice_fusion.5
  108.8 1.5 constant_dynamic-update-slice_fusion.4
  111.6 1.9 fusion.39
  113.5 1.9 fusion.38
  115.4 1.8 fusion.37
  117.2 1.8 fusion.36
  119.1 1.9 fusion.35
  120.9 1.9 fusion.34
  124.7 25.8 %reduce-scatter.2.cloned.1.call-done = bf16[128,2048]{1,0:T(8,128)(2,1)} async-done(((bf16[1024,2048]{1,0:T(8,128)(2,1)}), bf16[128,2048]{1,0:T(8,128)(2,1)}) %reduce-scatter.2.cloned.1.call-update) | async-done | bytes 524304 | tf_op jit(solution)/shard_map/reduce_scatter | solution.py:142
  151.7 11.7 %psum.36 = f32[128]{0:T(128)S(1)} all-reduce(f32[128]{0:T(128)S(1)} %get-tuple-element.34), channel_id=1, replica_groups=mesh['ctx'=8,'tp'=4] {'tp'}, use_global_device_ids=true, to_apply=%region_28.29 | all-reduce | flops 128 | bytes 1024 | tf_op jit(solution)/shard_map/psum | solution.py:45
  164.6 6.8 %fusion.70 = bf16[1,128,1024]{2,0,1:T(2,128)(2,1)S(1)} fusion(f32[1,255,1024]{2,0,1:T(1,128)} %copy-done.30, f32[128,1,1024]{2,0,1:T(8,128)S(1)} %bitcast.159), kind=kOutput, calls=%fused_computation.129 | convolution fusion | flops 201326592 | bytes 1830912 | tf_op jit(solution)/shard_map/conv_general_dilated | solution.py:29
  171.5 2.6 rev.15
  176.9 1.8 copy.104
  179.4 45.7 %all-reduce.3.cloned.1.call-done = bf16[128,1024]{1,0:T(8,128)(2,1)} async-done(((bf16[128,1024]{1,0:T(8,128)(2,1)}), bf16[128,1024]{1,0:T(8,128)(2,1)}) %all-reduce.3.cloned.1.call-update) | async-done | bytes 262160 | tf_op jit(solution)/shard_map/psum | solution.py:180
  225.1 1.8 convert_multiply_fusion.16
  227.1 5.8 %fusion.40 = f32[1,128,1024]{2,0,1:T(1,128)S(1)} fusion(f32[1,255,1024]{2,1,0:T(8,128)S(1)} %maximum_bitcast_fusion, f32[128,1,1024]{2,0,1:T(8,128)S(1)} %bitcast.164), kind=kOutput, calls=%fused_computation.77 | convolution fusion | flops 201326592 | bytes 2093056 | tf_op jit(solution)/shard_map/conv_general_dilated | solution.py:29
  232.9 2.7 %multiply_convert_fusion = (bf16[128,1024]{1,0:T(8,128)(2,1)}, f32[128,1024]{1,0:T(8,128)S(1)}, bf16[128,1024]{1,0:T(8,128)(2,1)}, bf16[128,1024]{1,0:T(8,128)(2,1)}, bf16[128,1024]{1,0:T(8,128)(2,1)}) fusion(f32[1,136,1024]{2,1,0:T(8,128)S(1)} %reshape.119, bf16[128,1024]{1,0:T(8,128)(2,1)S(1)} %copy-done.26, f32[1,128,1024]{2,0,1:T(1,128)S(1)} %fusion.40, ...), kind=kLoop, calls=%fused_computation.136 | loop fusion | flops 2621440 | bytes 4985856 | tf_op jit(solution)/shard_map/convert_element_type | solution.py:171
  237.1 22.4 %all-reduce = (bf16[7,1024]{1,0:T(8,128)(2,1)S(1)}, bf16[1024]{0:T(1024)(128)(2,1)S(1)}) all-reduce(bf16[7,1024]{1,0:T(8,128)(2,1)S(1)} %rev.14, bf16[1024]{0:T(1024)(128)(2,1)S(1)} %get-tuple-element.33), channel_id=1, replica_groups=mesh['ctx'=8,'tp'=4] {'ctx'}, use_global_device_ids=true, to_apply=%region_29.30 | all-reduce | flops 8192 | bytes 32768 | tf_op jit(solution)/shard_map/psum | solution.py:179
  (207 shorter events, 64.4 us)
Async XLA Ops:
  7.2 37.5 %all-gather.3.cloned.1.call-start = ((), (), s32[]{:S(2)}) async-start(), calls=%async_computation.1 | async-start | bytes 2359296 | tf_op jit(solution)/shard_map/all_gather | solution.py:85
  7.9 67.0 %all-gather.5.cloned.1.call-start = ((), (), s32[]{:S(2)}) async-start(), calls=%async_computation.2 | async-start | bytes 2359296 | tf_op jit(solution)/shard_map/all_gather | solution.py:86
  9.1 5.2 %collective-permute-start = (bf16[6,1024]{1,0:T(8,128)(2,1)S(1)}, bf16[6,1024]{1,0:T(8,128)(2,1)S(1)}, u32[]{:S(2)}, u32[]{:S(2)}) collective-permute-start(bf16[6,1024]{1,0:T(8,128)(2,1)S(1)} %slice.351), channel_id=1, source_target_pairs={{0,4},{4,8},{8,12},{12,16},{16,20},{20,24},{24,28},{1,5},{5,9},{9,... | collective-permute-start | bytes 36872 | tf_op jit(solution)/shard_map/ppermute | solution.py:25
  16.6 6.2 %copy-start.33 = (f32[128,1024]{1,0:T(8,128)S(1)}, f32[128,1024]{1,0:T(8,128)}, u32[]{:S(2)}) copy-start(f32[128,1024]{1,0:T(8,128)} %param.18) | copy-start | bytes 1572868
  17.4 5.8 %copy-start.1 = (bf16[128,1024]{1,0:T(8,128)(2,1)S(1)}, bf16[128,1024]{1,0:T(8,128)(2,1)}, u32[]{:S(2)}) copy-start(bf16[128,1024]{1,0:T(8,128)(2,1)} %param.23) | copy-start | bytes 786436
  17.4 5.9 %copy-start.36 = (bf16[128,1024]{1,0:T(8,128)(2,1)S(1)}, bf16[128,1024]{1,0:T(8,128)(2,1)}, u32[]{:S(2)}) copy-start(bf16[128,1024]{1,0:T(8,128)(2,1)} %param.20) | copy-start | bytes 786436
  17.4 6.8 %copy-start.39 = (s32[1024]{0:T(1024)S(1)}, s32[1024]{0:T(1024)}, u32[]{:S(2)}) copy-start(s32[1024]{0:T(1024)} %param.22) | copy-start | bytes 12292
  17.5 13.3 %copy-start.2 = (bf16[128,1024]{1,0:T(8,128)(2,1)}, bf16[128,1024]{1,0:T(8,128)(2,1)S(1)}, u32[]{:S(2)}) copy-start(bf16[128,1024]{1,0:T(8,128)(2,1)S(1)} %get-tuple-element.66) | copy-start | bytes 786436
  18.3 5.9 %collective-permute-start.1 = (bf16[127,1024]{1,0:T(8,128)(2,1)}, bf16[127,1024]{1,0:T(8,128)(2,1)S(1)}, u32[]{:S(2)}, u32[]{:S(2)}) collective-permute-start(bf16[127,1024]{1,0:T(8,128)(2,1)} %slice.349), channel_id=1, source_target_pairs={{0,4},{4,8},{8,12},{12,16},{16,20},{20,24},{24,28},{1,5},{5,9},{9,... | collective-permute-start | bytes 780296 | tf_op jit(solution)/shard_map/ppermute | solution.py:25
  25.1 5.7 %copy-start.30 = (f32[1,255,1024]{2,0,1:T(1,128)}, f32[1,255,1024]{2,0,1:T(1,128)S(1)}, u32[]{:S(2)}) copy-start(f32[1,255,1024]{2,0,1:T(1,128)S(1)} %broadcast_in_dim.33) | copy-start | bytes 3133444
  25.1 5.7 %copy-start.20 = (bf16[128,1024]{1,0:T(8,128)(2,1)S(1)}, bf16[128,1024]{1,0:T(8,128)(2,1)}, u32[]{:S(2)}) copy-start(bf16[128,1024]{1,0:T(8,128)(2,1)} %param.16) | copy-start | bytes 786436
  25.1 18.4 %copy-start.37 = (f32[1024]{0:T(1024)S(1)}, f32[1024]{0:T(1024)}, u32[]{:S(2)}) copy-start(f32[1024]{0:T(1024)} %param.19) | copy-start | bytes 12292
  44.4 106.1 %reduce-scatter.2.cloned.1.call-start = ((), (), s32[]{:S(2)}) async-start(), calls=%async_computation.3 | async-start | bytes 4718592 | tf_op jit(solution)/shard_map/reduce_scatter | solution.py:142
  67.3 14.2 %copy-start.4 = (bf16[128,1024]{1,0:T(8,128)(2,1)S(1)}, bf16[128,1024]{1,0:T(8,128)(2,1)}, u32[]{:S(2)}) copy-start(bf16[128,1024]{1,0:T(8,128)(2,1)} %get-tuple-element.60) | copy-start | bytes 786436
  74.9 5.4 %copy-start = (bf16[1024,1024]{1,0:T(8,128)(2,1)S(1)}, bf16[1024,1024]{1,0:T(8,128)(2,1)}, u32[]{:S(2)}) copy-start(bf16[1024,1024]{1,0:T(8,128)(2,1)} %all-gather.5.cloned.1.call-done) | copy-start | bytes 6291460
  74.9 6.9 %copy-start.24 = (bf16[128,1024]{1,0:T(8,128)(2,1)S(1)}, bf16[128,1024]{1,0:T(8,128)(2,1)}, u32[]{:S(2)}) copy-start(bf16[128,1024]{1,0:T(8,128)(2,1)} %get-tuple-element.62) | copy-start | bytes 786436
  74.9 7.3 %copy-start.10 = (bf16[128,1024]{1,0:T(8,128)(2,1)S(1)}, bf16[128,1024]{1,0:T(8,128)(2,1)}, u32[]{:S(2)}) copy-start(bf16[128,1024]{1,0:T(8,128)(2,1)} %get-tuple-element.48) | copy-start | bytes 786436
  83.1 3.9 %copy-start.7 = (bf16[128,1024]{1,0:T(8,128)(2,1)S(1)}, bf16[128,1024]{1,0:T(8,128)(2,1)}, u32[]{:S(2)}) copy-start(bf16[128,1024]{1,0:T(8,128)(2,1)} %get-tuple-element.54) | copy-start | bytes 786436
  84.1 3.9 %copy-start.8 = (bf16[128,1024]{1,0:T(8,128)(2,1)S(1)}, bf16[128,1024]{1,0:T(8,128)(2,1)}, u32[]{:S(2)}) copy-start(bf16[128,1024]{1,0:T(8,128)(2,1)} %get-tuple-element.52) | copy-start | bytes 786436
  99.0 12.6 %copy-start.17 = (bf16[1024,1024]{1,0:T(8,128)(2,1)S(1)}, bf16[1024,1024]{1,0:T(8,128)(2,1)}, u32[]{:S(2)}) copy-start(bf16[1024,1024]{1,0:T(8,128)(2,1)} %all-gather.3.cloned.1.call-done) | copy-start | bytes 6291460
  99.0 126.1 %all-reduce.3.cloned.1.call-start = ((), (), s32[]{:S(2)}) async-start(), calls=%async_computation.4 | async-start | bytes 524288 | tf_op jit(solution)/shard_map/psum | solution.py:180
  104.3 18.6 %copy-start.22 = (bf16[128,1024]{1,0:T(8,128)(2,1)S(1)}, bf16[128,1024]{1,0:T(8,128)(2,1)}, u32[]{:S(2)}) copy-start(bf16[128,1024]{1,0:T(8,128)(2,1)} %get-tuple-element.102) | copy-start | bytes 786436
  110.3 13.4 %copy-start.23 = (bf16[128,1024]{1,0:T(8,128)(2,1)S(1)}, bf16[128,1024]{1,0:T(8,128)(2,1)}, u32[]{:S(2)}) copy-start(bf16[128,1024]{1,0:T(8,128)(2,1)} %get-tuple-element.104) | copy-start | bytes 786436
  113.5 49.9 %copy-start.21 = (bf16[128,1024]{1,0:T(8,128)(2,1)S(1)}, bf16[128,1024]{1,0:T(8,128)(2,1)}, u32[]{:S(2)}) copy-start(bf16[128,1024]{1,0:T(8,128)(2,1)} %param.16) | copy-start | bytes 786436
  164.6 10.2 %copy-start.35 = (f32[128,128]{0,1:T(8,128)S(1)}, f32[128,128]{0,1:T(8,128)}, u32[]{:S(2)}) copy-start(f32[128,128]{0,1:T(8,128)} %get-tuple-element.88) | copy-start | bytes 196612
  171.4 7.2 %copy-start.18 = (bf16[128,2048]{1,0:T(8,128)(2,1)S(1)}, bf16[128,2048]{1,0:T(8,128)(2,1)}, u32[]{:S(2)}) copy-start(bf16[128,2048]{1,0:T(8,128)(2,1)} %reduce-scatter.2.cloned.1.call-done) | copy-start | bytes 1572868
  174.9 51.9 %collective-permute-start.2 = (bf16[127,1024]{1,0:T(8,128)(2,1)S(1)}, bf16[127,1024]{1,0:T(8,128)(2,1)S(1)}, u32[]{:S(2)}, u32[]{:S(2)}) collective-permute-start(bf16[127,1024]{1,0:T(8,128)(2,1)S(1)} %slice.348), channel_id=1, source_target_pairs={{4,0},{8,4},{12,8},{16,12},{20,16},{24,20},{28,24},{5,1},{9,5},{13... | collective-permute-start | bytes 780296 | tf_op jit(solution)/shard_map/ppermute | solution.py:25
  178.7 48.4 %copy-start.34 = (f32[128,1024]{1,0:T(8,128)S(1)}, f32[128,1024]{1,0:T(8,128)}, u32[]{:S(2)}) copy-start(f32[128,1024]{1,0:T(8,128)} %param.18) | copy-start | bytes 1572868
  227.0 5.8 %copy-start.3 = (bf16[128,1024]{1,0:T(8,128)(2,1)S(1)}, bf16[128,1024]{1,0:T(8,128)(2,1)}, u32[]{:S(2)}) copy-start(bf16[128,1024]{1,0:T(8,128)(2,1)} %copy-done.2) | copy-start | bytes 786436
  227.1 5.8 %copy-start.16 = (f32[1,128,1024]{2,0,1:T(1,128)S(1)}, f32[1,128,1024]{2,0,1:T(1,128)}, u32[]{:S(2)}) copy-start(f32[1,128,1024]{2,0,1:T(1,128)} %copy-done.15) | copy-start | bytes 1572868
  227.1 5.8 %copy-start.26 = (bf16[128,1024]{1,0:T(8,128)(2,1)S(1)}, bf16[128,1024]{1,0:T(8,128)(2,1)}, u32[]{:S(2)}) copy-start(bf16[128,1024]{1,0:T(8,128)(2,1)} %param.17) | copy-start | bytes 786436
  260.1 3.1 %collective-permute-start.3 = (bf16[6,1024]{1,0:T(8,128)(2,1)S(1)}, bf16[6,1024]{1,0:T(8,128)(2,1)S(1)}, u32[]{:S(2)}, u32[]{:S(2)}) collective-permute-start(bf16[6,1024]{1,0:T(8,128)(2,1)S(1)} %slice.350), channel_id=1, source_target_pairs={{4,0},{8,4},{12,8},{16,12},{20,16},{24,20},{28,24},{5,1},{9,5},{13... | collective-permute-start | bytes 36872 | tf_op jit(solution)/shard_map/ppermute | solution.py:25
  (17 other events, 31.2 us)
Sparse Core Ops, SparseCore 0:
  9.9 30.5 all-gather.2
  44.5 30.3 all-gather.4
  99.1 51.3 reduce-scatter.1
  174.3 50.7 all-reduce.2
where the time goes:
time: 274 us; the launch traced here: 273 us
  waiting for transfers between devices  81 us (30%)
  matrix products  60.8 us (22%)
  blocking collectives  46 us (17%)
  local copies, waits for them, and re-layouts  35.2 us (13%)
  other arithmetic  25.2 us (9%)
  between operations  14.6 us (5%)
  starting transfers between devices  10 us (4%)
    psum x1, waiting for transfers between devices, shards(): lax.psum(kernel_part.astype(jnp.bfloat16), 'ctx').astype(jnp.float32)  45.7 us
    reduce_scatter x1, waiting for transfers between devices, shards(): lax.psum_scatter(jnp.concatenate([key_part.reshape(local_rows * lax.axis_...  25.8 us
    psum x2, blocking collectives, channel_total(): return lax.psum(partial_value, 'tp')  23.6 us
    psum x1, blocking collectives, shards(): lax.psum(stencil_part.astype(jnp.bfloat16), 'ctx').astype(jnp.float32)  22.4 us
    conv_general_dilated x6, matrix products, depthwise(): lax.conv_general_dilated(padded[None], tap_rows[:, None, :], (1,), 'VALID...  19.9 us
    dot_general x8, matrix products, shards(): query_grad = jnp.dot(dscore, key_head, preferred_element_type=jnp.float32)  13 us
    unnamed x93, local copies, waits for them, and re-layouts  12.7 us
    dot_general x8, matrix products, shards(): lax.dot_general(query_head, key_head, contract, preferred_element_type=jn...  10.6 us
  transfers between devices with their start and end apart: 8, of which 4 were waited for; matrix products, arithmetic and copies ran while one was open for 25% of the time, Pallas kernels for 0%

commit v1 on v0

--- a/solution.py
+++ b/solution.py
@@ -9,6 +9,18 @@
 KS = 7
 KM = 128
 epsilon = 1e-06
+
+
+def doubled_up(array, axis, dim):
+    ways, here = (lax.axis_size(axis), lax.axis_index(axis))
+    grown, reach = (array, 1)
+    while reach < ways:
+        theirs = lax.ppermute(grown, axis, [(d, d ^ reach) for d in range(ways)])
+        mine_first = jnp.concatenate([grown, theirs], axis=dim)
+        theirs_first = jnp.concatenate([theirs, grown], axis=dim)
+        grown = jnp.where(here & reach == 0, mine_first, theirs_first)
+        reach = 2 * reach
+    return grown
 
 
 def as_sent(shard):
@@ -83,7 +95,7 @@
     normed = (second_wide * inverse_rms[:, None] * scaling).astype(jnp.bfloat16)
     keys_whole, values_whole = (
         lax.all_gather(matchers, "ctx", axis=0, tiled=True),
-        lax.all_gather(normed, "ctx", axis=0, tiled=True),
+        doubled_up(normed, "ctx", 0),
     )
     query_pos = position + jnp.arange(local_rows, dtype=jnp.int32)
     key_pos = jnp.arange(total_rows, dtype=jnp.int32)

time: 274 us -> 304 us (1.11)
  waiting for transfers between devices: 81 us -> 107 us
  starting transfers between devices: 10 us -> 18.6 us
    ppermute x0 -> x3, waiting for transfers between devices: none -> 34.1 us  [doubled_up(): theirs = lax.ppermute(grown, axis, [(d, d ^ reach) for d in range(ways)])]
    ppermute x0 -> x3, starting transfers between devices: none -> 8.99 us  [doubled_up(): theirs = lax.ppermute(grown, axis, [(d, d ^ reach) for d in range(ways)])]
    all_gather x1 -> x0, waiting for transfers between devices: 7.58 us -> none  [shards(): lax.all_gather(normed, 'ctx', axis=0, tiled=True)]
    unnamed x7, other arithmetic: 5.92 us -> 1.02 us
    dot_general x8, matrix products: 8.07 us -> 3.21 us  [shards(): attended = jnp.dot(weights, value_head, preferred_element_type=jnp.float32)]
    select_n x0 -> x3, other arithmetic: none -> 3.95 us  [doubled_up(): grown = jnp.where(here & reach == 0, mine_first, theirs_first)]
    unnamed x93 -> x95, local copies, waits for them, and re-layouts: 12.7 us -> 11.9 us
  transfers between devices with their start and end apart: 8 -> 10, of which waited for: 4 -> 7; matrix products, arithmetic and copies ran while one was open for 25% -> 15% of each run, Pallas kernels for 0% -> 0%
where the time goes in v1:
time: 304 us; the launch traced here: 302 us
  waiting for transfers between devices  107 us (35%)
  matrix products  58.7 us (19%)
  blocking collectives  46.3 us (15%)
  local copies, waits for them, and re-layouts  34.5 us (11%)
  other arithmetic  22.8 us (8%)
  starting transfers between devices  18.6 us (6%)
  between operations  14.8 us (5%)
    psum x1, waiting for transfers between devices, shards(): lax.psum(kernel_part.astype(jnp.bfloat16), 'ctx').astype(jnp.float32)  45.7 us
    ppermute x3, waiting for transfers between devices, doubled_up(): theirs = lax.ppermute(grown, axis, [(d, d ^ reach) for d in range(ways)])  34.1 us
    reduce_scatter x1, waiting for transfers between devices, shards(): lax.psum_scatter(jnp.concatenate([key_part.reshape(local_rows * lax.axis_...  24.9 us
    psum x2, blocking collectives, channel_total(): return lax.psum(partial_value, 'tp')  23.9 us
    psum x1, blocking collectives, shards(): lax.psum(stencil_part.astype(jnp.bfloat16), 'ctx').astype(jnp.float32)  22.4 us
    conv_general_dilated x6, matrix products, depthwise(): lax.conv_general_dilated(padded[None], tap_rows[:, None, :], (1,), 'VALID...  21.1 us
    dot_general x8, matrix products, shards(): query_grad = jnp.dot(dscore, key_head, preferred_element_type=jnp.float32)  13 us
    unnamed x95, local copies, waits for them, and re-layouts  11.9 us
  transfers between devices with their start and end apart: 10, of which 7 were waited for; matrix products, arithmetic and copies ran while one was open for 15% of the time, Pallas kernels for 0%

profile of v1, /device:TPU:0, one launch (start us, length us, event | category | flops | bytes accessed | tf_op | source)
XLA Modules:
  0.0 302.3 jit_solution(16478012472475460625)
XLA Ops:
  8.3 2.4 collective-permute-start
  10.7 2.8 rev.12
  16.8 4.5 %collective-permute-start.1 = (bf16[127,1024]{1,0:T(8,128)(2,1)S(1)}, bf16[127,1024]{1,0:T(8,128)(2,1)S(1)}, u32[]{:S(2)}, u32[]{:S(2)}) collective-permute-start(bf16[127,1024]{1,0:T(8,128)(2,1)S(1)} %slice.349), channel_id=1, source_target_pairs={{0,4},{4,8},{8,12},{12,16},{16,20},{20,24},{24,28},{1,5},{5,9},{9,... | collective-permute-start | bytes 780296 | tf_op jit(solution)/shard_map/ppermute | solution.py:37
  23.4 5.6 %fusion.74 = f32[1,128,1024]{2,0,1:T(1,128)S(1)} fusion(f32[1,255,1024]{2,0,1:T(1,128)S(1)} %broadcast_in_dim.33, f32[128,1,1024]{2,0,1:T(8,128)S(1)} %bitcast.165), kind=kOutput, calls=%fused_computation.136 | convolution fusion | flops 201326592 | bytes 2093056 | tf_op jit(solution)/shard_map/conv_general_dilated | solution.py:41
  29.9 12.2 %psum.35 = f32[128]{0:T(128)S(1)} all-reduce(f32[128]{0:T(128)S(1)} %get-tuple-element.63), channel_id=1, replica_groups=mesh['ctx'=8,'tp'=4] {'tp'}, use_global_device_ids=true, to_apply=%region_3.4 | all-reduce | flops 128 | bytes 1024 | tf_op jit(solution)/shard_map/psum | solution.py:57
  44.1 4.8 %collective-permute-start.3 = (bf16[256,1024]{1,0:T(8,128)(2,1)S(1)}, bf16[256,1024]{1,0:T(8,128)(2,1)S(1)}, u32[]{:S(2)}, u32[]{:S(2)}) collective-permute-start(bf16[256,1024]{1,0:T(8,128)(2,1)S(1)} %maximum_select_fusion.2), channel_id=1, source_target_pairs={{0,8},{4,12},{8,0},{12,4},{16,24},{20,28},{24,16},{28,20},{1,9},{5... | collective-permute-start | bytes 1572872 | tf_op jit(solution)/shard_map/ppermute | solution.py:18
  48.9 12.2 %collective-permute-done.3 = bf16[256,1024]{1,0:T(8,128)(2,1)S(1)} collective-permute-done((bf16[256,1024]{1,0:T(8,128)(2,1)S(1)}, bf16[256,1024]{1,0:T(8,128)(2,1)S(1)}, u32[]{:S(2)}, u32[]{:S(2)}) %collective-permute-start.3) | collective-permute-done | bytes 524320 | tf_op jit(solution)/shard_map/ppermute | solution.py:18
  61.6 3.6 %collective-permute-start.4 = (bf16[512,1024]{1,0:T(8,128)(2,1)S(1)}, bf16[512,1024]{1,0:T(8,128)(2,1)}, u32[]{:S(2)}, u32[]{:S(2)}) collective-permute-start(bf16[512,1024]{1,0:T(8,128)(2,1)S(1)} %maximum_select_fusion.1), channel_id=1, source_target_pairs={{0,16},{4,20},{8,24},{12,28},{16,0},{20,4},{24,8},{28,12},{1,17},{... | collective-permute-start | bytes 3145736 | tf_op jit(solution)/shard_map/ppermute | solution.py:18
  65.4 1.8 copy.113
  67.3 20.7 %collective-permute-done.4 = bf16[512,1024]{1,0:T(8,128)(2,1)} collective-permute-done((bf16[512,1024]{1,0:T(8,128)(2,1)S(1)}, bf16[512,1024]{1,0:T(8,128)(2,1)}, u32[]{:S(2)}, u32[]{:S(2)}) %collective-permute-start.4) | collective-permute-done | bytes 1048608 | tf_op jit(solution)/shard_map/ppermute | solution.py:18
  88.0 3.3 %maximum_select_fusion = bf16[1024,1024]{1,0:T(8,128)(2,1)S(1)} fusion(bf16[512,1024]{1,0:T(8,128)(2,1)} %collective-permute-done.4, bf16[512,1024]{1,0:T(8,128)(2,1)} %copy-done, pred[]{:T(512)S(6)} %eq.25), kind=kLoop, calls=%fused_computation.1 | loop fusion | flops 9437184 | bytes 4194305 | tf_op jit(solution)/shard_map/jit(_where)/select_n | solution.py:21
  117.1 2.6 copy.114
  119.7 2.3 convolution_convert_fusion
  122.0 2.6 copy.116
  124.6 4.7 %pad_maximum_fusion = bf16[1024,2048]{1,0:T(8,128)(2,1)} fusion(bf16[1024,1024]{1,0:T(8,128)(2,1)} %copy.116, bf16[1024,1024]{1,0:T(8,128)(2,1)} %copy.114), kind=kLoop, calls=%fused_computation | loop fusion | flops 8388608 | bytes 8388608 | tf_op jit(solution)/shard_map/concatenate | solution.py:155
  129.4 1.7 copy.67
  140.8 1.9 fusion.39
  142.7 1.9 fusion.38
  144.6 1.8 fusion.37
  146.4 1.8 fusion.36
  148.3 1.8 fusion.35
  150.1 1.9 fusion.34
  153.8 24.9 %reduce-scatter.2.cloned.1.call-done = bf16[128,2048]{1,0:T(8,128)(2,1)} async-done(((bf16[1024,2048]{1,0:T(8,128)(2,1)}), bf16[128,2048]{1,0:T(8,128)(2,1)}) %reduce-scatter.2.cloned.1.call-update) | async-done | bytes 524304 | tf_op jit(solution)/shard_map/reduce_scatter | solution.py:154
  179.8 11.7 %psum.36 = f32[128]{0:T(128)S(1)} all-reduce(f32[128]{0:T(128)S(1)} %get-tuple-element.34), channel_id=1, replica_groups=mesh['ctx'=8,'tp'=4] {'tp'}, use_global_device_ids=true, to_apply=%region_28.29 | all-reduce | flops 128 | bytes 1024 | tf_op jit(solution)/shard_map/psum | solution.py:57
  192.8 6.8 %fusion.70 = bf16[1,128,1024]{2,0,1:T(2,128)(2,1)S(1)} fusion(f32[1,255,1024]{2,0,1:T(1,128)} %copy-done.24, f32[128,1,1024]{2,0,1:T(8,128)S(1)} %bitcast.159), kind=kOutput, calls=%fused_computation.132 | convolution fusion | flops 201326592 | bytes 1830912 | tf_op jit(solution)/shard_map/conv_general_dilated | solution.py:41
  199.8 2.6 rev.15
  205.1 1.8 copy.104
  207.6 45.7 %all-reduce.3.cloned.1.call-done = bf16[128,1024]{1,0:T(8,128)(2,1)} async-done(((bf16[128,1024]{1,0:T(8,128)(2,1)}), bf16[128,1024]{1,0:T(8,128)(2,1)}) %all-reduce.3.cloned.1.call-update) | async-done | bytes 262160 | tf_op jit(solution)/shard_map/psum | solution.py:192
  253.3 1.8 convert_multiply_fusion.16
  255.3 7.0 %fusion.40 = f32[1,128,1024]{2,0,1:T(1,128)S(1)} fusion(f32[1,255,1024]{2,1,0:T(8,128)S(1)} %maximum_bitcast_fusion, f32[128,1,1024]{2,0,1:T(8,128)} %bitcast.164), kind=kOutput, calls=%fused_computation.79 | convolution fusion | flops 201326592 | bytes 2093056 | tf_op jit(solution)/shard_map/conv_general_dilated | solution.py:41
  262.4 2.7 multiply_convert_fusion
  266.6 22.4 %all-reduce = (bf16[7,1024]{1,0:T(8,128)(2,1)S(1)}, bf16[1024]{0:T(1024)(128)(2,1)S(1)}) all-reduce(bf16[7,1024]{1,0:T(8,128)(2,1)S(1)} %rev.14, bf16[1024]{0:T(1024)(128)(2,1)S(1)} %get-tuple-element.33), channel_id=1, replica_groups=mesh['ctx'=8,'tp'=4] {'ctx'}, use_global_device_ids=true, to_apply=%region_29.30 | all-reduce | flops 8192 | bytes 32768 | tf_op jit(solution)/shard_map/psum | solution.py:191
  (215 shorter events, 61.1 us)
Async XLA Ops:
  7.2 84.2 %all-gather.2.cloned.1.call-start = ((), (), s32[]{:S(2)}) async-start(), calls=%async_computation.1 | async-start | bytes 2359296 | tf_op jit(solution)/shard_map/all_gather | solution.py:97
  8.3 5.2 %collective-permute-start = (bf16[6,1024]{1,0:T(8,128)(2,1)S(1)}, bf16[6,1024]{1,0:T(8,128)(2,1)S(1)}, u32[]{:S(2)}, u32[]{:S(2)}) collective-permute-start(bf16[6,1024]{1,0:T(8,128)(2,1)S(1)} %slice.351), channel_id=1, source_target_pairs={{0,4},{4,8},{8,12},{12,16},{16,20},{20,24},{24,28},{1,5},{5,9},{9,... | collective-permute-start | bytes 36872 | tf_op jit(solution)/shard_map/ppermute | solution.py:37
  15.9 5.6 %copy-start.35 = (f32[128,1024]{1,0:T(8,128)S(1)}, f32[128,1024]{1,0:T(8,128)}, u32[]{:S(2)}) copy-start(f32[128,1024]{1,0:T(8,128)} %param.18) | copy-start | bytes 1572868
  16.8 12.3 %copy-start.3 = (bf16[128,1024]{1,0:T(8,128)(2,1)}, bf16[128,1024]{1,0:T(8,128)(2,1)S(1)}, u32[]{:S(2)}) copy-start(bf16[128,1024]{1,0:T(8,128)(2,1)S(1)} %get-tuple-element.66) | copy-start | bytes 786436
  16.8 5.7 %collective-permute-start.1 = (bf16[127,1024]{1,0:T(8,128)(2,1)S(1)}, bf16[127,1024]{1,0:T(8,128)(2,1)S(1)}, u32[]{:S(2)}, u32[]{:S(2)}) collective-permute-start(bf16[127,1024]{1,0:T(8,128)(2,1)S(1)} %slice.349), channel_id=1, source_target_pairs={{0,4},{4,8},{8,12},{12,16},{16,20},{20,24},{24,28},{1,5},{5,9},{9,... | collective-permute-start | bytes 780296 | tf_op jit(solution)/shard_map/ppermute | solution.py:37
  21.4 157.3 %reduce-scatter.2.cloned.1.call-start = ((), (), s32[]{:S(2)}) async-start(), calls=%async_computation.2 | async-start | bytes 4718592 | tf_op jit(solution)/shard_map/reduce_scatter | solution.py:154
  23.4 5.7 %copy-start.24 = (f32[1,255,1024]{2,0,1:T(1,128)}, f32[1,255,1024]{2,0,1:T(1,128)S(1)}, u32[]{:S(2)}) copy-start(f32[1,255,1024]{2,0,1:T(1,128)S(1)} %broadcast_in_dim.33) | copy-start | bytes 3133444
  23.4 5.7 %copy-start.15 = (bf16[128,1024]{1,0:T(8,128)(2,1)S(1)}, bf16[128,1024]{1,0:T(8,128)(2,1)}, u32[]{:S(2)}) copy-start(bf16[128,1024]{1,0:T(8,128)(2,1)} %param.16) | copy-start | bytes 786436
  23.4 18.7 %copy-start.38 = (f32[1024]{0:T(1024)S(1)}, f32[1024]{0:T(1024)}, u32[]{:S(2)}) copy-start(f32[1024]{0:T(1024)} %param.19) | copy-start | bytes 12292
  29.9 35.4 %copy-start.2 = (bf16[128,1024]{1,0:T(8,128)(2,1)S(1)}, bf16[128,1024]{1,0:T(8,128)(2,1)}, u32[]{:S(2)}) copy-start(bf16[128,1024]{1,0:T(8,128)(2,1)} %param.23) | copy-start | bytes 786436
  42.2 1.7 collective-permute-start.2
  42.8 24.4 %copy-start.40 = (s32[1024]{0:T(1024)S(1)}, s32[1024]{0:T(1024)}, u32[]{:S(2)}) copy-start(s32[1024]{0:T(1024)} %param.22) | copy-start | bytes 12292
  44.1 17.0 %collective-permute-start.3 = (bf16[256,1024]{1,0:T(8,128)(2,1)S(1)}, bf16[256,1024]{1,0:T(8,128)(2,1)S(1)}, u32[]{:S(2)}, u32[]{:S(2)}) collective-permute-start(bf16[256,1024]{1,0:T(8,128)(2,1)S(1)} %maximum_select_fusion.2), channel_id=1, source_target_pairs={{0,8},{4,12},{8,0},{12,4},{16,24},{20,28},{24,16},{28,20},{1,9},{5... | collective-permute-start | bytes 1572872 | tf_op jit(solution)/shard_map/ppermute | solution.py:18
  61.6 5.7 %copy-start = (bf16[512,1024]{1,0:T(8,128)(2,1)}, bf16[512,1024]{1,0:T(8,128)(2,1)S(1)}, u32[]{:S(2)}) copy-start(bf16[512,1024]{1,0:T(8,128)(2,1)S(1)} %maximum_select_fusion.1) | copy-start | bytes 3145732
  61.6 26.4 %collective-permute-start.4 = (bf16[512,1024]{1,0:T(8,128)(2,1)S(1)}, bf16[512,1024]{1,0:T(8,128)(2,1)}, u32[]{:S(2)}, u32[]{:S(2)}) collective-permute-start(bf16[512,1024]{1,0:T(8,128)(2,1)S(1)} %maximum_select_fusion.1), channel_id=1, source_target_pairs={{0,16},{4,20},{8,24},{12,28},{16,0},{20,4},{24,8},{28,12},{1,17},{... | collective-permute-start | bytes 3145736 | tf_op jit(solution)/shard_map/ppermute | solution.py:18
  107.3 4.2 %copy-start.1 = (bf16[8,128,1024]{2,1,0:T(8,128)(2,1)}, bf16[8,128,1024]{2,1,0:T(8,128)(2,1)S(1)}, u32[]{:S(2)}) copy-start(bf16[8,128,1024]{2,1,0:T(8,128)(2,1)S(1)} %get-tuple-element.47) | copy-start | bytes 6291460
  129.3 4.2 %copy-start.28 = (f32[128,128]{0,1:T(8,128)S(1)}, f32[128,128]{0,1:T(8,128)}, u32[]{:S(2)}) copy-start(f32[128,128]{0,1:T(8,128)} %copy-done.27) | copy-start | bytes 196612
  129.3 4.3 %copy-start.26 = (f32[128,128]{0,1:T(8,128)S(1)}, f32[128,128]{0,1:T(8,128)}, u32[]{:S(2)}) copy-start(f32[128,128]{0,1:T(8,128)} %copy-done.25) | copy-start | bytes 196612
  129.3 11.6 %copy-start.11 = (bf16[1024,1024]{1,0:T(8,128)(2,1)S(1)}, bf16[1024,1024]{1,0:T(8,128)(2,1)}, u32[]{:S(2)}) copy-start(bf16[1024,1024]{1,0:T(8,128)(2,1)} %all-gather.2.cloned.1.call-done) | copy-start | bytes 6291460
  129.3 124.0 %all-reduce.3.cloned.1.call-start = ((), (), s32[]{:S(2)}) async-start(), calls=%async_computation.3 | async-start | bytes 524288 | tf_op jit(solution)/shard_map/psum | solution.py:192
  134.4 17.6 %copy-start.17 = (bf16[128,1024]{1,0:T(8,128)(2,1)S(1)}, bf16[128,1024]{1,0:T(8,128)(2,1)}, u32[]{:S(2)}) copy-start(bf16[128,1024]{1,0:T(8,128)(2,1)} %get-tuple-element.102) | copy-start | bytes 786436
  139.6 13.3 %copy-start.18 = (bf16[128,1024]{1,0:T(8,128)(2,1)S(1)}, bf16[128,1024]{1,0:T(8,128)(2,1)}, u32[]{:S(2)}) copy-start(bf16[128,1024]{1,0:T(8,128)(2,1)} %get-tuple-element.104) | copy-start | bytes 786436
  142.7 48.9 %copy-start.16 = (bf16[128,1024]{1,0:T(8,128)(2,1)S(1)}, bf16[128,1024]{1,0:T(8,128)(2,1)}, u32[]{:S(2)}) copy-start(bf16[128,1024]{1,0:T(8,128)(2,1)} %param.16) | copy-start | bytes 786436
  192.8 9.6 %copy-start.37 = (f32[128,128]{1,0:T(8,128)S(1)}, f32[128,128]{1,0:T(8,128)}, u32[]{:S(2)}) copy-start(f32[128,128]{1,0:T(8,128)} %copy.73) | copy-start | bytes 196612
  192.8 10.2 %copy-start.36 = (f32[128,128]{0,1:T(8,128)S(1)}, f32[128,128]{0,1:T(8,128)}, u32[]{:S(2)}) copy-start(f32[128,128]{0,1:T(8,128)} %get-tuple-element.88) | copy-start | bytes 196612
  199.7 7.2 %copy-start.12 = (bf16[128,2048]{1,0:T(8,128)(2,1)S(1)}, bf16[128,2048]{1,0:T(8,128)(2,1)}, u32[]{:S(2)}) copy-start(bf16[128,2048]{1,0:T(8,128)(2,1)} %reduce-scatter.2.cloned.1.call-done) | copy-start | bytes 1572868
  203.2 51.9 %collective-permute-start.5 = (bf16[127,1024]{1,0:T(8,128)(2,1)S(1)}, bf16[127,1024]{1,0:T(8,128)(2,1)S(1)}, u32[]{:S(2)}, u32[]{:S(2)}) collective-permute-start(bf16[127,1024]{1,0:T(8,128)(2,1)S(1)} %slice.348), channel_id=1, source_target_pairs={{4,0},{8,4},{12,8},{16,12},{20,16},{24,20},{28,24},{5,1},{9,5},{13... | collective-permute-start | bytes 780296 | tf_op jit(solution)/shard_map/ppermute | solution.py:37
  255.3 7.0 %copy-start.4 = (bf16[128,1024]{1,0:T(8,128)(2,1)S(1)}, bf16[128,1024]{1,0:T(8,128)(2,1)}, u32[]{:S(2)}) copy-start(bf16[128,1024]{1,0:T(8,128)(2,1)} %copy-done.3) | copy-start | bytes 786436
  255.3 7.0 %copy-start.10 = (f32[1,128,1024]{2,0,1:T(1,128)S(1)}, f32[1,128,1024]{2,0,1:T(1,128)}, u32[]{:S(2)}) copy-start(f32[1,128,1024]{2,0,1:T(1,128)} %copy-done.9) | copy-start | bytes 1572868
  255.3 7.0 %copy-start.13 = (bf16[128,2048]{1,0:T(8,128)(2,1)S(1)}, bf16[128,2048]{1,0:T(8,128)(2,1)}, u32[]{:S(2)}) copy-start(bf16[128,2048]{1,0:T(8,128)(2,1)} %reduce-scatter.2.cloned.1.call-done) | copy-start | bytes 1572868
  255.3 7.0 %copy-start.20 = (bf16[128,1024]{1,0:T(8,128)(2,1)S(1)}, bf16[128,1024]{1,0:T(8,128)(2,1)}, u32[]{:S(2)}) copy-start(bf16[128,1024]{1,0:T(8,128)(2,1)} %param.17) | copy-start | bytes 786436
  289.6 3.1 %collective-permute-start.6 = (bf16[6,1024]{1,0:T(8,128)(2,1)S(1)}, bf16[6,1024]{1,0:T(8,128)(2,1)S(1)}, u32[]{:S(2)}, u32[]{:S(2)}) collective-permute-start(bf16[6,1024]{1,0:T(8,128)(2,1)S(1)} %slice.350), channel_id=1, source_target_pairs={{4,0},{8,4},{12,8},{16,12},{20,16},{24,20},{28,24},{5,1},{9,5},{13... | collective-permute-start | bytes 36872 | tf_op jit(solution)/shard_map/ppermute | solution.py:37
  (20 other events, 45.2 us)
Sparse Core Ops, SparseCore 0:
  21.5 29.0 all-gather.1
  129.4 49.2 reduce-scatter.1
  202.5 50.7 all-reduce.2
